TPU v7x, 512 devices: a whole 4x8x8 slice. The times are simulated.
512 devices in a mesh: dp: 4 (over y_lo, core), seq: 4 (over x), fsdp: 32 (over y_hi, z).
Axes of the slice: x: 4, y: 8 (y_hi: 4, y_lo: 2; y = y_hi * 2 + y_lo), z: 8, core: 2. Of those that a mesh axis runs over, the one named last changes fastest.
Arguments:
- patches: bfloat16 [128, 768, 6144], P(('dp', 'fsdp'), 'seq'), may hold values from -100 to 100
- segments: int32 [128, 768], P(('dp', 'fsdp'), 'seq'), may hold values from 0 to 7, never falling along the last dimension, each value on 1 to 384 neighbouring positions
- qkv_weight: bfloat16 [6144, 384], P('fsdp'), may hold values from -0.078125 to 0.078125
- cotangent: bfloat16 [128, 768, 128], P(('dp', 'fsdp'), 'seq'), may hold values from -6 to 6
Outputs:
- input_grad: bfloat16 [128, 768, 6144], P(('dp', 'fsdp'), 'seq')
- weight_grad: float32 [6144, 384], P('fsdp')
Inputs may be any that keep to these rules, and one draw needn't show every extreme that they name: `segments`: within a sequence the image number never falls; each of the 8 images has 1 to 384 patches and one has exactly 384.
All inputs are finite; a program needn't handle non-finite values.
Results may differ from a plain program's by a relative error of at most 0.034.
The roundings to bfloat16 on the way count: a program that leaves them out, or rounds other values in their place, can miss the bound.
Values may be sent and summed in bfloat16 or wider, within the bound.
No kernel may reach another device: no remote copies, remote signals or barrier semaphores. Data moves between devices by JAX's collectives and lax.ppermute only.
A program may use at most 64 MiB of HBM per device.

v0:
```python
import jax
import jax.numpy as jnp
from jax import lax
from jax.sharding import PartitionSpec as P


def contract_first(left, right):
    return lax.dot_general(
        left, right, (((0,), (0,)), ((), ())), preferred_element_type=jnp.float32
    )


def contract_last(left, right):
    return lax.dot_general(
        left, right, (((1,), (1,)), ((), ())), preferred_element_type=jnp.float32
    )


def shards(patches, segments, qkv_weight, cotangent):
    features = patches[0]
    image_ids = segments[0]
    grad_out = cotangent[0]
    width_head = cotangent.shape[2]
    scale = width_head ** (-0.5)
    full_weight = lax.all_gather(qkv_weight, "fsdp", axis=0, tiled=True)
    projected = jnp.dot(features, full_weight, preferred_element_type=jnp.float32)
    heads = projected.astype(jnp.bfloat16)
    query = heads[:, :width_head]
    own_pairs = heads[:, width_head:]
    pairs_all, images_all = (
        lax.all_gather(own_pairs, "seq", axis=0, tiled=True),
        lax.all_gather(image_ids, "seq", axis=0, tiled=True),
    )
    keys_all = pairs_all[:, :width_head]
    values_all = pairs_all[:, width_head:]
    scores = contract_last(query, keys_all) * scale
    allowed = image_ids[:, None] == images_all[None, :]
    highest = jnp.max(jnp.where(allowed, scores, -jnp.inf), axis=1)
    summed = jnp.sum(jnp.where(allowed, jnp.exp(scores - highest[:, None]), 0.0), axis=1)
    log_total = highest + jnp.log(summed)
    attention = jnp.where(allowed, jnp.exp(scores - log_total[:, None]), 0.0)
    attention_low = attention.astype(jnp.bfloat16)
    output = jnp.dot(attention_low, values_all, preferred_element_type=jnp.float32)
    delta_rows = jnp.sum(grad_out.astype(jnp.float32) * output, axis=1)
    grad_attention = contract_last(grad_out, values_all)
    grad_scores = (attention * (grad_attention - delta_rows[:, None]) * scale).astype(jnp.bfloat16)
    grad_query = jnp.dot(grad_scores, keys_all, preferred_element_type=jnp.float32).astype(
        jnp.bfloat16
    )
    partial_pairs = jnp.concatenate(
        [contract_first(grad_scores, query), contract_first(attention_low, grad_out)], axis=1
    )
    grad_pairs = lax.psum_scatter(
        partial_pairs.astype(jnp.bfloat16), "seq", scatter_dimension=0, tiled=True
    )
    grad_heads = jnp.concatenate([grad_query, grad_pairs], axis=1)
    columns = lax.all_to_all(features, "fsdp", split_axis=1, concat_axis=0, tiled=True)
    partial_grad = contract_first(columns, lax.all_gather(grad_heads, "fsdp", axis=0, tiled=True))
    input_grad = contract_last(grad_heads, full_weight).astype(jnp.bfloat16)
    weight_grad = lax.psum(partial_grad.astype(jnp.bfloat16), ("dp", "seq")).astype(jnp.float32)
    return (input_grad[None], weight_grad)


def solution(mesh):
    placed = (
        P(("dp", "fsdp"), "seq", None),
        P(("dp", "fsdp"), "seq"),
        P("fsdp", None),
        P(("dp", "fsdp"), "seq", None),
    )
    return jax.shard_map(
        shards,
        mesh=mesh,
        in_specs=placed,
        out_specs=(P(("dp", "fsdp"), "seq", None), P("fsdp", None)),
        check_vma=False,
    )
```

profile of v0, /device:TPU:1, one launch (start us, length us, event | category | flops | bytes accessed | tf_op | source)
XLA Modules:
  0.0 472.2 jit_solution(8760330779892001765)
XLA Ops:
  7.2 0.7 all-gather.4.cloned.1.call-update
  7.9 1.3 dynamic-slice
  9.9 0.9 dynamic-update-slice
  10.8 7.7 %all-reduce = s32[768]{0:T(1024)S(1)} all-reduce(s32[768]{0:T(1024)S(1)} %dynamic-update-slice), channel_id=2, replica_groups=mesh['dp'=4,'seq'=4,'fsdp'=32] {'seq'}, use_global_device_ids=true, to_apply=%add | all-reduce | flops 768 | bytes 6144
  18.5 103.9 %all-gather.4.cloned.1.call-done = bf16[6144,384]{1,0:T(8,128)(2,1)} async-done(((bf16[192,384]{1,0:T(8,128)(2,1)}), bf16[6144,384]{1,0:T(8,128)(2,1)}) %all-gather.4.cloned.1.call-update) | async-done | bytes 4718608 | tf_op jit(solution)/shard_map/all_gather | solution.py:25
  122.4 4.4 fusion.7
  126.8 9.9 %all_gather.14 = bf16[768,256]{1,0:T(8,128)(2,1)S(1)} all-gather(bf16[192,256]{1,0:T(8,128)(2,1)S(1)} %slice.17), channel_id=1, replica_groups=mesh['dp'=4,'seq'=4,'fsdp'=32] {'seq'}, dimensions={0}, use_global_device_ids=true | all-gather | bytes 491520 | tf_op jit(solution)/shard_map/all_gather | solution.py:31
  136.8 0.3 fusion.12
  137.1 0.3 fusion.13
  137.9 0.3 fusion.11
  138.2 0.3 fusion.6
  138.8 0.9 copy.13
  140.1 23.7 %reduce-scatter.4.cloned.1.call-done = bf16[192,256]{1,0:T(8,128)(2,1)} async-done(((bf16[768,256]{1,0:T(8,128)(2,1)}), bf16[192,256]{1,0:T(8,128)(2,1)}) %reduce-scatter.4.cloned.1.call-update) | async-done | bytes 98320
  163.9 1.0 copy.14
  164.9 0.8 copy.10
  165.8 3.0 copy.11
  168.8 104.7 %all_to_all.19 = bf16[192,32,192]{0,2,1:T(8,128)(2,1)S(1)} all-to-all(bf16[192,32,192]{0,2,1:T(8,128)(2,1)S(1)} %bitcast.39), channel_id=1, replica_groups=mesh['dp'=4,'seq'=4,'fsdp'=32] {'fsdp'}, dimensions={1} | all-to-all | bytes 4718592 | tf_op jit(solution)/shard_map/all_to_all | solution.py:57
  273.5 1.8 copy.12
  275.2 4.2 all_to_all.17
  279.5 57.0 %all-gather.6.cloned.1.call-done = bf16[6144,384]{1,0:T(8,128)(2,1)} async-done(((bf16[192,384]{1,0:T(8,128)(2,1)}), bf16[6144,384]{1,0:T(8,128)(2,1)}) %all-gather.6.cloned.1.call-update) | async-done | bytes 4718608 | tf_op jit(solution)/shard_map/all_gather | solution.py:58
  336.4 5.1 %fusion.10 = bf16[192,384]{1,0:T(8,128)(2,1)} fusion(bf16[6144,192]{0,1:T(8,128)(2,1)} %all_to_all.17, bf16[6144,384]{1,0:T(8,128)(2,1)} %all-gather.6.cloned.1.call-done), kind=kOutput, calls=%fused_computation.14 | convolution fusion | flops 906043392 | bytes 7225344 | tf_op jit(solution)/shard_map/dot_general | solution.py:8
  341.5 5.6 %fusion = bf16[1,192,6144]{2,1,0:T(8,128)(2,1)} fusion(bf16[6144,384]{1,0:T(8,128)(2,1)} %all-gather.4.cloned.1.call-done, bf16[192,256]{0,1:T(8,128)(2,1)S(1)} %copy.14, bf16[192,128]{0,1:T(8,128)(2,1)S(1)} %copy.9), kind=kOutput, calls=%fused_computation.1 | convolution fusion | flops 907444224 | bytes 7225344 | tf_op jit(solution)/shard_map/dot_general | solution.py:14
  347.2 116.8 %all-reduce.3.cloned.1.call-done = bf16[192,384]{1,0:T(8,128)(2,1)} async-done(((bf16[192,384]{1,0:T(8,128)(2,1)}), bf16[192,384]{1,0:T(8,128)(2,1)}) %all-reduce.3.cloned.1.call-update) | async-done | bytes 147472 | tf_op jit(solution)/shard_map/psum | solution.py:60
  464.0 1.6 convert_element_type.36
  (21 shorter events, 1.3 us)
Async XLA Ops:
  7.2 115.2 %all-gather.4.cloned.1.call-start = ((), (), s32[]{:S(2)}) async-start(), calls=%async_computation.2 | async-start | bytes 4866048 | tf_op jit(solution)/shard_map/all_gather | solution.py:25
  7.9 156.0 %reduce-scatter.4.cloned.1.call-start = ((), (), s32[]{:S(2)}) async-start(), calls=%async_computation.5 | async-start | bytes 491520
  18.5 118.3 %copy-start.1 = (s32[1,192]{1,0:T(1,128)S(1)}, s32[1,192]{1,0:T(1,128)}, u32[]{:S(2)}) copy-start(s32[1,192]{1,0:T(1,128)} %param.5) | copy-start | bytes 2308
  126.8 10.8 %copy-start = (bf16[1,192,128]{2,1,0:T(8,128)(2,1)S(1)}, bf16[1,192,128]{2,1,0:T(8,128)(2,1)}, u32[]{:S(2)}) copy-start(bf16[1,192,128]{2,1,0:T(8,128)(2,1)} %param.7) | copy-start | bytes 147460
  139.7 196.7 %all-gather.6.cloned.1.call-start = ((), (), s32[]{:S(2)}) async-start(), calls=%async_computation.3 | async-start | bytes 4866048 | tf_op jit(solution)/shard_map/all_gather | solution.py:58
  165.7 298.3 %all-reduce.3.cloned.1.call-start = ((), (), s32[]{:S(2)}) async-start(), calls=%async_computation.4 | async-start | bytes 294912 | tf_op jit(solution)/shard_map/psum | solution.py:60
Sparse Core Ops, SparseCore 0:
  11.2 111.1 all-gather.3
  139.9 23.9 reduce-scatter.3
  168.1 168.2 all-gather.5
  341.7 122.2 all-reduce.2
where the time goes:
time: 473 us; the launch traced here: 472 us
  waiting for transfers between devices  302 us (64%)
  blocking collectives  122 us (26%)
  matrix products  16.9 us (4%)
  between operations  14.5 us (3%)
  local copies, waits for them, and re-layouts  14 us (3%)
    psum x1, waiting for transfers between devices, shards(): lax.psum(partial_grad.astype(jnp.bfloat16), ('dp', 'seq'))  117 us
    all_to_all x1, blocking collectives, shards(): lax.all_to_all(features, 'fsdp', split_axis=1, concat_axis=0, tiled=True)  105 us
    all_gather x1, waiting for transfers between devices, shards(): full_weight = lax.all_gather(qkv_weight, 'fsdp', axis=0, tiled=True)  104 us
    all_gather x1, waiting for transfers between devices, shards(): lax.all_gather(grad_heads, 'fsdp', axis=0, tiled=True)  57 us
    unnamed x5, waiting for transfers between devices  24.5 us
    all_gather x1, blocking collectives, shards(): lax.all_gather(own_pairs, 'seq', axis=0, tiled=True)  9.94 us
  transfers between devices with their start and end apart: 4, of which 4 were waited for; matrix products, arithmetic and copies ran while one was open for 3% of the time, Pallas kernels for 0%

commit v1 on v0

--- a/solution.py
+++ b/solution.py
@@ -17,6 +17,12 @@
 
 
 def shards(patches, segments, qkv_weight, cotangent):
+
+    def write_routes_all_for(incoming_x):
+        for kk in ("seq", "dp"):
+            incoming_x = lax.psum(incoming_x, axis_name=kk)
+        return incoming_x
+
     features = patches[0]
     image_ids = segments[0]
     grad_out = cotangent[0]
@@ -57,7 +63,7 @@
     columns = lax.all_to_all(features, "fsdp", split_axis=1, concat_axis=0, tiled=True)
     partial_grad = contract_first(columns, lax.all_gather(grad_heads, "fsdp", axis=0, tiled=True))
     input_grad = contract_last(grad_heads, full_weight).astype(jnp.bfloat16)
-    weight_grad = lax.psum(partial_grad.astype(jnp.bfloat16), ("dp", "seq")).astype(jnp.float32)
+    weight_grad = write_routes_all_for(partial_grad.astype(jnp.bfloat16)).astype(jnp.float32)
     return (input_grad[None], weight_grad)
 
 

time: 473 us -> 449 us (0.949)
  waiting for transfers between devices: 302 us -> 279 us
    psum x1 -> x2, waiting for transfers between devices: 117 us -> 93.3 us  [write_routes_all_for(): incoming_x = lax.psum(incoming_x, axis_name=kk)]
    unnamed x5 -> x6, waiting for transfers between devices: 24.5 us -> 24.5 us
  transfers between devices with their start and end apart: 4 -> 5, of which waited for: 4 -> 5; matrix products, arithmetic and copies ran while one was open for 3% -> 3% of each run, Pallas kernels for 0% -> 0%
where the time goes in v1:
time: 449 us
  waiting for transfers between devices  279 us (62%)
  blocking collectives  122 us (27%)
  matrix products  16.9 us (4%)
  between operations  14.6 us (3%)
  local copies, waits for them, and re-layouts  14 us (3%)
    all_to_all x1, blocking collectives, shards(): lax.all_to_all(features, 'fsdp', split_axis=1, concat_axis=0, tiled=True)  105 us
    all_gather x1, waiting for transfers between devices, shards(): full_weight = lax.all_gather(qkv_weight, 'fsdp', axis=0, tiled=True)  104 us
    psum x2, waiting for transfers between devices, write_routes_all_for(): incoming_x = lax.psum(incoming_x, axis_name=kk)  93.3 us
    all_gather x1, waiting for transfers between devices, shards(): lax.all_gather(grad_heads, 'fsdp', axis=0, tiled=True)  57 us
    unnamed x6, waiting for transfers between devices  24.5 us
    all_gather x1, blocking collectives, shards(): lax.all_gather(own_pairs, 'seq', axis=0, tiled=True)  9.94 us
  transfers between devices with their start and end apart: 5, of which 5 were waited for; matrix products, arithmetic and copies ran while one was open for 3% of the time, Pallas kernels for 0%

profile of v1, /device:TPU:1, one launch (start us, length us, event | category | flops | bytes accessed | tf_op | source)
XLA Modules:
  0.0 448.7 jit_solution(16543935629076641330)
XLA Ops:
  7.2 0.7 all-gather.4.cloned.1.call-update
  7.9 1.3 dynamic-slice
  9.9 0.9 dynamic-update-slice
  10.8 7.7 %all-reduce = s32[768]{0:T(1024)S(1)} all-reduce(s32[768]{0:T(1024)S(1)} %dynamic-update-slice), channel_id=2, replica_groups=mesh['dp'=4,'seq'=4,'fsdp'=32] {'seq'}, use_global_device_ids=true, to_apply=%add | all-reduce | flops 768 | bytes 6144
  18.5 103.9 %all-gather.4.cloned.1.call-done = bf16[6144,384]{1,0:T(8,128)(2,1)} async-done(((bf16[192,384]{1,0:T(8,128)(2,1)}), bf16[6144,384]{1,0:T(8,128)(2,1)}) %all-gather.4.cloned.1.call-update) | async-done | bytes 4718608 | tf_op jit(solution)/shard_map/all_gather | solution.py:31
  122.4 4.4 fusion.7
  126.8 9.9 %all_gather.14 = bf16[768,256]{1,0:T(8,128)(2,1)S(1)} all-gather(bf16[192,256]{1,0:T(8,128)(2,1)S(1)} %slice.17), channel_id=1, replica_groups=mesh['dp'=4,'seq'=4,'fsdp'=32] {'seq'}, dimensions={0}, use_global_device_ids=true | all-gather | bytes 491520 | tf_op jit(solution)/shard_map/all_gather | solution.py:37
  136.8 0.3 fusion.12
  137.9 0.3 fusion.11
  138.2 0.3 fusion.6
  138.8 0.9 copy.13
  140.1 23.7 %reduce-scatter.4.cloned.1.call-done = bf16[192,256]{1,0:T(8,128)(2,1)} async-done(((bf16[768,256]{1,0:T(8,128)(2,1)}), bf16[192,256]{1,0:T(8,128)(2,1)}) %reduce-scatter.4.cloned.1.call-update) | async-done | bytes 98320
  163.9 1.0 copy.14
  164.9 0.8 copy.10
  165.8 3.0 copy.11
  168.8 104.6 %all_to_all.19 = bf16[192,32,192]{0,2,1:T(8,128)(2,1)S(1)} all-to-all(bf16[192,32,192]{0,2,1:T(8,128)(2,1)S(1)} %bitcast.39), channel_id=1, replica_groups=mesh['dp'=4,'seq'=4,'fsdp'=32] {'fsdp'}, dimensions={1} | all-to-all | bytes 4718592 | tf_op jit(solution)/shard_map/all_to_all | solution.py:63
  273.4 1.8 copy.12
  275.2 4.2 all_to_all.17
  279.4 57.0 %all-gather.6.cloned.1.call-done = bf16[6144,384]{1,0:T(8,128)(2,1)} async-done(((bf16[192,384]{1,0:T(8,128)(2,1)}), bf16[6144,384]{1,0:T(8,128)(2,1)}) %all-gather.6.cloned.1.call-update) | async-done | bytes 4718608 | tf_op jit(solution)/shard_map/all_gather | solution.py:64
  336.4 5.1 %fusion.10 = bf16[192,384]{1,0:T(8,128)(2,1)} fusion(bf16[6144,192]{0,1:T(8,128)(2,1)} %all_to_all.17, bf16[6144,384]{1,0:T(8,128)(2,1)} %all-gather.6.cloned.1.call-done), kind=kOutput, calls=%fused_computation.14 | convolution fusion | flops 906043392 | bytes 7225344 | tf_op jit(solution)/shard_map/dot_general | solution.py:8
  341.6 47.6 %all-reduce.4.cloned.1.call-done = bf16[192,384]{1,0:T(8,128)(2,1)} async-done(((bf16[192,384]{1,0:T(8,128)(2,1)}), bf16[192,384]{1,0:T(8,128)(2,1)}) %all-reduce.4.cloned.1.call-update) | async-done | bytes 147472 | tf_op jit(solution)/shard_map/psum | solution.py:23
  389.2 5.6 %fusion = bf16[1,192,6144]{2,1,0:T(8,128)(2,1)} fusion(bf16[6144,384]{1,0:T(8,128)(2,1)} %all-gather.4.cloned.1.call-done, bf16[192,256]{0,1:T(8,128)(2,1)S(1)} %copy.14, bf16[192,128]{0,1:T(8,128)(2,1)S(1)} %copy.9), kind=kOutput, calls=%fused_computation.1 | convolution fusion | flops 907444224 | bytes 7225344 | tf_op jit(solution)/shard_map/dot_general | solution.py:14
  394.8 45.7 %all-reduce.6.cloned.1.call-done = bf16[192,384]{1,0:T(8,128)(2,1)} async-done(((bf16[192,384]{1,0:T(8,128)(2,1)}), bf16[192,384]{1,0:T(8,128)(2,1)}) %all-reduce.6.cloned.1.call-update) | async-done | bytes 147472 | tf_op jit(solution)/shard_map/psum | solution.py:23
  440.5 1.6 convert_element_type.36
  (24 shorter events, 1.7 us)
Async XLA Ops:
  7.2 115.2 %all-gather.4.cloned.1.call-start = ((), (), s32[]{:S(2)}) async-start(), calls=%async_computation.2 | async-start | bytes 4866048 | tf_op jit(solution)/shard_map/all_gather | solution.py:31
  7.9 156.0 %reduce-scatter.4.cloned.1.call-start = ((), (), s32[]{:S(2)}) async-start(), calls=%async_computation.6 | async-start | bytes 491520
  18.5 118.3 %copy-start.1 = (s32[1,192]{1,0:T(1,128)S(1)}, s32[1,192]{1,0:T(1,128)}, u32[]{:S(2)}) copy-start(s32[1,192]{1,0:T(1,128)} %param.5) | copy-start | bytes 2308
  126.8 10.8 %copy-start = (bf16[1,192,128]{2,1,0:T(8,128)(2,1)S(1)}, bf16[1,192,128]{2,1,0:T(8,128)(2,1)}, u32[]{:S(2)}) copy-start(bf16[1,192,128]{2,1,0:T(8,128)(2,1)} %param.7) | copy-start | bytes 147460
  139.7 196.7 %all-gather.6.cloned.1.call-start = ((), (), s32[]{:S(2)}) async-start(), calls=%async_computation.3 | async-start | bytes 4866048 | tf_op jit(solution)/shard_map/all_gather | solution.py:64
  165.7 223.5 %all-reduce.4.cloned.1.call-start = ((), (), s32[]{:S(2)}) async-start(), calls=%async_computation.4 | async-start | bytes 294912 | tf_op jit(solution)/shard_map/psum | solution.py:23
  341.5 99.0 %all-reduce.6.cloned.1.call-start = ((), (), s32[]{:S(2)}) async-start(), calls=%async_computation.5 | async-start | bytes 294912 | tf_op jit(solution)/shard_map/psum | solution.py:23
Sparse Core Ops, SparseCore 0:
  11.2 111.1 all-gather.3
  139.9 23.9 reduce-scatter.3
  168.1 168.2 all-gather.5
  341.6 47.4 all-reduce.3
  392.0 48.5 all-reduce.5
